TPU v7x, 32 devices: a whole 2x2x4 slice. The times are simulated.
32 devices in a mesh: section: 4 (over y, x), expert: 8 (over z, core).
Axes of the slice: x: 2, y: 2, z: 4, core: 2. Of those that a mesh axis runs over, the one named last changes fastest.
Arguments:
- tokens: bfloat16 [4, 128, 2048], P(None, 'expert'), may hold values from -6 to 6
- norm_gain: float32 [4, 2048], P('section'), may hold values from 0.1 to 1.9
- gate_weight: bfloat16 [4, 16, 2048, 768], P('section', 'expert'), may hold values from -0.125 to 0.125
- up_weight: bfloat16 [4, 16, 2048, 768], P('section', 'expert'), may hold values from -0.125 to 0.125
- down_weight: bfloat16 [4, 16, 768, 2048], P('section', 'expert'), may hold values from -0.21875 to 0.21875
- routes: int32 [4, 4, 128, 8], P('section', None, 'expert'), may hold values from 0 to 15, all different within a row; in each aligned block of 16 rows (0 to 15, 16 to 31, ..., all dimensions but the last counted through in order) at most 12 rows name the same one
- gates: float32 [4, 4, 128, 8], P('section', None, 'expert'), may hold values from 0.1 to 1
Outputs:
- hidden_states: bfloat16 [4, 4, 128, 2048], P('section', None, 'expert')
Inputs may be any that keep to these rules, and one draw needn't show every extreme that they name: `routes`: within one section and micro-batch, the 16 tokens of one device name any one expert at most 12 times, a bound that some expert reaches in some of these blocks; the 8 experts of a token differ.
All inputs are finite; a program needn't handle non-finite values.
Results may differ from a plain program's by a relative error of at most 0.012.
Values may be sent and summed in bfloat16 or wider, within the bound.
No kernel may reach another device: no remote copies, remote signals or barrier semaphores. Data moves between devices by JAX's collectives and lax.ppermute only.
A program may use at most 128 MiB of HBM per device.

v0:
```python
import jax
import jax.numpy as jnp
from jax import lax
from jax.sharding import PartitionSpec as P

MB = 4
EPSILON = 1e-06


def shifted(array, axis, by):
    count = lax.axis_size(axis)
    pairs = [(i, i + by) for i in range(count) if 0 <= i + by < count]
    return lax.ppermute(array, axis, pairs)


def place_slots(expert_ids, experts):
    onehot = (expert_ids[:, None] == jnp.arange(experts, dtype=jnp.int32)[None, :]).astype(
        jnp.int32
    )
    before = jnp.cumsum(onehot, axis=0) - onehot
    return jnp.sum(before * onehot, axis=1)


def rms_normed(hidden, gain):
    values = hidden.astype(jnp.float32)
    scale = lax.rsqrt(jnp.mean(values * values, axis=-1, keepdims=True) + EPSILON)
    return (values, (values * scale * gain).astype(jnp.bfloat16))


def on_device(tokens, norm_gain, gate_weight, up_weight, down_weight, routes, gates):
    devices = lax.axis_size("expert")
    sections = lax.axis_size("section")
    section_index = lax.axis_index("section")
    local_experts = gate_weight.shape[1]
    experts = local_experts * devices
    tok_rows = tokens.shape[1]
    width = tokens.shape[2]
    topk = routes.shape[3]
    capacity = tok_rows * topk * 3 // (2 * experts)
    gain = norm_gain[0]
    w_gate = gate_weight[0]
    w_up = up_weight[0]
    w_down = down_weight[0]
    held = jnp.zeros((tok_rows, width), jnp.bfloat16)
    collected = jnp.zeros((MB, tok_rows, width), jnp.bfloat16)
    for moment in range(MB + sections - 1):
        if moment > 0:
            arrived = shifted(held, "section", 1)
        else:
            arrived = held
        batch_index = moment - section_index
        active = (batch_index >= 0) & (batch_index < MB)
        clipped = jnp.clip(batch_index, 0, MB - 1)
        first_rows = lax.dynamic_index_in_dim(tokens, clipped, 0, keepdims=False)
        incoming = jnp.where(section_index == 0, first_rows, arrived)
        expert_ids = lax.dynamic_index_in_dim(routes[0], clipped, 0, keepdims=False)
        gate_values = lax.dynamic_index_in_dim(gates[0], clipped, 0, keepdims=False)
        values, normed = rms_normed(incoming, gain)
        flat_ids = expert_ids.reshape(-1)
        slot_index = place_slots(flat_ids, experts)
        token_index = jnp.arange(tok_rows * topk, dtype=jnp.int32) // topk
        outgoing = jnp.zeros((experts, capacity, width), jnp.bfloat16)
        outgoing = outgoing.at[flat_ids, slot_index].set(normed[token_index])
        outgoing = outgoing.reshape(devices, local_experts, capacity, width)
        received = lax.all_to_all(outgoing, "expert", split_axis=0, concat_axis=0, tiled=True)
        gate_part = jnp.einsum(
            "nesd,edf->nesf", received, w_gate, preferred_element_type=jnp.float32
        )
        up_part = jnp.einsum("nesd,edf->nesf", received, w_up, preferred_element_type=jnp.float32)
        inner = (jax.nn.silu(gate_part) * up_part).astype(jnp.bfloat16)
        returned = lax.all_to_all(
            jnp.einsum("nesf,efd->nesd", inner, w_down, preferred_element_type=jnp.float32).astype(
                jnp.bfloat16
            ),
            "expert",
            split_axis=0,
            concat_axis=0,
            tiled=True,
        )
        returned = returned.reshape(experts, capacity, width)
        picked = returned[flat_ids, slot_index].reshape(tok_rows, topk, width)
        weights = gate_values / jnp.sum(gate_values, axis=-1, keepdims=True)
        mixed = jnp.sum(weights[:, :, None] * picked.astype(jnp.float32), axis=1)
        produced = (values + mixed).astype(jnp.bfloat16)
        held = jnp.where(active, produced, incoming)
        updated = lax.dynamic_update_index_in_dim(collected, held, clipped, 0)
        collected = jnp.where(active, updated, collected)
    return collected[None]


def solution(mesh):
    placed = (
        P(None, "expert", None),
        P("section", None),
        P("section", "expert", None, None),
        P("section", "expert", None, None),
        P("section", "expert", None, None),
        P("section", None, "expert", None),
        P("section", None, "expert", None),
    )
    return jax.shard_map(
        on_device,
        mesh=mesh,
        in_specs=placed,
        out_specs=P("section", None, "expert", None),
        check_vma=False,
    )
```

profile of v0, /device:TPU:4, one launch (start us, length us, event | category | flops | bytes accessed | tf_op | source)
XLA Modules:
  0.0 598.4 jit_solution(2576998763865678790)
XLA Ops:
  5.2 11.8 %scatter_fusion = bf16[16,12,2048]{2,0,1:T(8,128)(2,1)S(1)} fusion(bf16[16,12,2048]{2,0,1:T(8,128)(2,1)S(1)} %broadcast.475.clone, s32[128]{0:T(128)S(1)} %get-tuple-element.46, bf16[128,2048]{1,0:T(8,128)(2,1)S(1)} %gather_fusion), kind=kCustom, calls=%fused_computation.14 | custom fusion | bytes 1573888 | tf_op jit(solution)/shard_map/scatter | solution.py:63
  18.1 25.7 %all_to_all.70 = bf16[8,2,12,2048]{3,1,2,0:T(2,128)(2,1)S(1)} all-to-all(bf16[8,2,12,2048]{3,1,2,0:T(2,128)(2,1)S(1)} %copy.67), channel_id=1, replica_groups=mesh['section'=4,'expert'=8] {'expert'}, dimensions={0} | all-to-all | bytes 1572864 | tf_op jit(solution)/shard_map/all_to_all | solution.py:65
  47.8 6.8 %fusion.81 = bf16[8,2,12,2048]{3,2,0,1:T(8,128)(2,1)S(1)} fusion(bf16[1,2,768,2048]{3,2,1,0:T(8,128)(2,1)} %param.11, bf16[1,2,2048,768]{3,2,1,0:T(8,128)(2,1)} %param.10, bf16[8,2,12,2048]{3,1,2,0:T(2,128)(2,1)S(1)} %all_to_all.70, f32[8,2,12,768]{3,2,0,1:T(8,128)S(1)} %fusion.84), kind=kOutput, calls=%fused_computation.76 | convolution fusion | flops 1209237504 | bytes 14745600 | tf_op jit(solution)/shard_map/nesf,efd->nesd/dot_general | solution.py:72
  60.0 20.7 %all-to-all-done.1 = bf16[8,2,12,2048]{3,1,2,0:T(2,128)(2,1)S(1)} async-done(((bf16[8,2,12,2048]{3,1,2,0:T(2,128)(2,1)}), bf16[8,2,12,2048]{3,1,2,0:T(2,128)(2,1)S(1)}, u32[]{:S(2)}, u32[]{:S(2)}) %all-to-all-start.1) | async-done | bytes 786464 | tf_op jit(solution)/shard_map/all_to_all | solution.py:71
  92.9 11.8 %scatter_fusion.1 = bf16[16,12,2048]{2,0,1:T(8,128)(2,1)S(1)} fusion(bf16[16,12,2048]{2,0,1:T(8,128)(2,1)S(1)} %broadcast.475.clone.1, s32[128]{0:T(128)S(1)} %get-tuple-element.62, bf16[128,2048]{1,0:T(8,128)(2,1)S(1)} %gather_fusion.2), kind=kCustom, calls=%fused_computation.15 | custom fusion | bytes 1573888 | tf_op jit(solution)/shard_map/scatter | solution.py:63
  105.9 23.4 %all_to_all.71 = bf16[8,2,12,2048]{3,1,2,0:T(2,128)(2,1)S(1)} all-to-all(bf16[8,2,12,2048]{3,1,2,0:T(2,128)(2,1)S(1)} %copy.75), channel_id=1, replica_groups=mesh['section'=4,'expert'=8] {'expert'}, dimensions={0} | all-to-all | bytes 1572864 | tf_op jit(solution)/shard_map/all_to_all | solution.py:65
  133.2 6.7 %fusion.78 = bf16[8,2,12,2048]{3,2,0,1:T(8,128)(2,1)S(1)} fusion(bf16[1,2,768,2048]{3,2,1,0:T(8,128)(2,1)} %param.11, bf16[1,2,2048,768]{3,2,1,0:T(8,128)(2,1)} %param.10, bf16[8,2,12,2048]{3,1,2,0:T(2,128)(2,1)S(1)} %all_to_all.71, f32[8,2,12,768]{3,2,0,1:T(8,128)S(1)} %fusion.87), kind=kOutput, calls=%fused_computation.75 | convolution fusion | flops 1209237504 | bytes 14745600 | tf_op jit(solution)/shard_map/nesf,efd->nesd/dot_general | solution.py:72
  146.8 19.3 %all-to-all-done.3 = bf16[8,2,12,2048]{3,1,2,0:T(2,128)(2,1)S(1)} async-done(((bf16[8,2,12,2048]{3,1,2,0:T(2,128)(2,1)}), bf16[8,2,12,2048]{3,1,2,0:T(2,128)(2,1)S(1)}, u32[]{:S(2)}, u32[]{:S(2)}) %all-to-all-start.3) | async-done | bytes 786464 | tf_op jit(solution)/shard_map/all_to_all | solution.py:71
  178.4 11.8 %scatter_fusion.2 = bf16[16,12,2048]{2,0,1:T(8,128)(2,1)S(1)} fusion(bf16[16,12,2048]{2,0,1:T(8,128)(2,1)S(1)} %broadcast.475.clone.2, s32[128]{0:T(128)S(1)} %get-tuple-element.38, bf16[128,2048]{1,0:T(8,128)(2,1)S(1)} %gather_fusion.4), kind=kCustom, calls=%fused_computation.16 | custom fusion | bytes 1573888 | tf_op jit(solution)/shard_map/scatter | solution.py:63
  191.3 23.4 %all_to_all.72 = bf16[8,2,12,2048]{3,1,2,0:T(2,128)(2,1)S(1)} all-to-all(bf16[8,2,12,2048]{3,1,2,0:T(2,128)(2,1)S(1)} %copy.83), channel_id=1, replica_groups=mesh['section'=4,'expert'=8] {'expert'}, dimensions={0} | all-to-all | bytes 1572864 | tf_op jit(solution)/shard_map/all_to_all | solution.py:65
  218.6 6.8 %fusion.75 = bf16[8,2,12,2048]{3,2,0,1:T(8,128)(2,1)S(1)} fusion(bf16[1,2,768,2048]{3,2,1,0:T(8,128)(2,1)} %param.11, bf16[1,2,2048,768]{3,2,1,0:T(8,128)(2,1)} %param.10, bf16[8,2,12,2048]{3,1,2,0:T(2,128)(2,1)S(1)} %all_to_all.72, f32[8,2,12,768]{3,2,0,1:T(8,128)S(1)} %fusion.90), kind=kOutput, calls=%fused_computation.74 | convolution fusion | flops 1209237504 | bytes 14745600 | tf_op jit(solution)/shard_map/nesf,efd->nesd/dot_general | solution.py:72
  230.8 20.8 %all-to-all-done.5 = bf16[8,2,12,2048]{3,1,2,0:T(2,128)(2,1)S(1)} async-done(((bf16[8,2,12,2048]{3,1,2,0:T(2,128)(2,1)}), bf16[8,2,12,2048]{3,1,2,0:T(2,128)(2,1)S(1)}, u32[]{:S(2)}, u32[]{:S(2)}) %all-to-all-start.5) | async-done | bytes 786464 | tf_op jit(solution)/shard_map/all_to_all | solution.py:71
  257.6 4.9 collective-permute-done.2
  263.8 11.8 %scatter_fusion.3 = bf16[16,12,2048]{2,0,1:T(8,128)(2,1)S(1)} fusion(bf16[16,12,2048]{2,0,1:T(8,128)(2,1)S(1)} %broadcast.475.clone.3, s32[128]{0:T(128)S(1)} %get-tuple-element.64, bf16[128,2048]{1,0:T(8,128)(2,1)S(1)} %gather_fusion.6), kind=kCustom, calls=%fused_computation.17 | custom fusion | bytes 1573888 | tf_op jit(solution)/shard_map/scatter | solution.py:63
  276.8 23.4 %all_to_all.73 = bf16[8,2,12,2048]{3,1,2,0:T(2,128)(2,1)S(1)} all-to-all(bf16[8,2,12,2048]{3,1,2,0:T(2,128)(2,1)S(1)} %copy.91), channel_id=1, replica_groups=mesh['section'=4,'expert'=8] {'expert'}, dimensions={0} | all-to-all | bytes 1572864 | tf_op jit(solution)/shard_map/all_to_all | solution.py:65
  304.2 6.7 %fusion.72 = bf16[8,2,12,2048]{3,2,0,1:T(8,128)(2,1)S(1)} fusion(bf16[1,2,768,2048]{3,2,1,0:T(8,128)(2,1)} %param.11, bf16[1,2,2048,768]{3,2,1,0:T(8,128)(2,1)} %param.10, bf16[8,2,12,2048]{3,1,2,0:T(2,128)(2,1)S(1)} %all_to_all.73, f32[8,2,12,768]{3,2,0,1:T(8,128)S(1)} %fusion.93), kind=kOutput, calls=%fused_computation.73 | convolution fusion | flops 1209237504 | bytes 14745600 | tf_op jit(solution)/shard_map/nesf,efd->nesd/dot_general | solution.py:72
  317.6 19.4 %all-to-all-done.7 = bf16[8,2,12,2048]{3,1,2,0:T(2,128)(2,1)S(1)} async-done(((bf16[8,2,12,2048]{3,1,2,0:T(2,128)(2,1)}), bf16[8,2,12,2048]{3,1,2,0:T(2,128)(2,1)S(1)}, u32[]{:S(2)}, u32[]{:S(2)}) %all-to-all-start.7) | async-done | bytes 786464 | tf_op jit(solution)/shard_map/all_to_all | solution.py:71
  343.3 4.7 collective-permute-done.3
  349.3 11.9 %scatter_fusion.4 = bf16[16,12,2048]{2,0,1:T(8,128)(2,1)S(1)} fusion(bf16[16,12,2048]{2,0,1:T(8,128)(2,1)S(1)} %broadcast.475.clone.4, s32[128]{0:T(128)S(1)} %get-tuple-element.26, bf16[128,2048]{1,0:T(8,128)(2,1)S(1)} %gather_fusion.8), kind=kCustom, calls=%fused_computation.18 | custom fusion | bytes 1573888 | tf_op jit(solution)/shard_map/scatter | solution.py:63
  362.2 23.4 %all_to_all.74 = bf16[8,2,12,2048]{3,1,2,0:T(2,128)(2,1)S(1)} all-to-all(bf16[8,2,12,2048]{3,1,2,0:T(2,128)(2,1)S(1)} %copy.99), channel_id=1, replica_groups=mesh['section'=4,'expert'=8] {'expert'}, dimensions={0} | all-to-all | bytes 1572864 | tf_op jit(solution)/shard_map/all_to_all | solution.py:65
  389.6 6.8 %fusion.69 = bf16[8,2,12,2048]{3,2,0,1:T(8,128)(2,1)S(1)} fusion(bf16[1,2,768,2048]{3,2,1,0:T(8,128)(2,1)} %param.11, bf16[1,2,2048,768]{3,2,1,0:T(8,128)(2,1)} %param.10, bf16[8,2,12,2048]{3,1,2,0:T(2,128)(2,1)S(1)} %all_to_all.74, f32[8,2,12,768]{3,2,0,1:T(8,128)S(1)} %fusion.96), kind=kOutput, calls=%fused_computation.72 | convolution fusion | flops 1209237504 | bytes 14745600 | tf_op jit(solution)/shard_map/nesf,efd->nesd/dot_general | solution.py:72
  401.7 20.8 %all-to-all-done.9 = bf16[8,2,12,2048]{3,1,2,0:T(2,128)(2,1)S(1)} async-done(((bf16[8,2,12,2048]{3,1,2,0:T(2,128)(2,1)}), bf16[8,2,12,2048]{3,1,2,0:T(2,128)(2,1)S(1)}, u32[]{:S(2)}, u32[]{:S(2)}) %all-to-all-start.9) | async-done | bytes 786464 | tf_op jit(solution)/shard_map/all_to_all | solution.py:71
  428.5 5.0 collective-permute-done.4
  434.8 11.8 %scatter_fusion.5 = bf16[16,12,2048]{2,0,1:T(8,128)(2,1)S(1)} fusion(bf16[16,12,2048]{2,0,1:T(8,128)(2,1)S(1)} %broadcast.475.clone.5, s32[128]{0:T(128)S(1)} %get-tuple-element.66, bf16[128,2048]{1,0:T(8,128)(2,1)S(1)} %gather_fusion.10), kind=kCustom, calls=%fused_computation.19 | custom fusion | bytes 1573888 | tf_op jit(solution)/shard_map/scatter | solution.py:63
  447.8 23.4 %all_to_all.75 = bf16[8,2,12,2048]{3,1,2,0:T(2,128)(2,1)S(1)} all-to-all(bf16[8,2,12,2048]{3,1,2,0:T(2,128)(2,1)S(1)} %copy.107), channel_id=1, replica_groups=mesh['section'=4,'expert'=8] {'expert'}, dimensions={0} | all-to-all | bytes 1572864 | tf_op jit(solution)/shard_map/all_to_all | solution.py:65
  475.1 6.8 %fusion.66 = bf16[8,2,12,2048]{3,2,0,1:T(8,128)(2,1)S(1)} fusion(bf16[1,2,768,2048]{3,2,1,0:T(8,128)(2,1)} %param.11, bf16[1,2,2048,768]{3,2,1,0:T(8,128)(2,1)} %param.10, bf16[8,2,12,2048]{3,1,2,0:T(2,128)(2,1)S(1)} %all_to_all.75, f32[8,2,12,768]{3,2,0,1:T(8,128)S(1)} %fusion.99), kind=kOutput, calls=%fused_computation.71 | convolution fusion | flops 1209237504 | bytes 14745600 | tf_op jit(solution)/shard_map/nesf,efd->nesd/dot_general | solution.py:72
  487.9 20.1 %all-to-all-done.11 = bf16[8,2,12,2048]{3,1,2,0:T(2,128)(2,1)S(1)} async-done(((bf16[8,2,12,2048]{3,1,2,0:T(2,128)(2,1)}), bf16[8,2,12,2048]{3,1,2,0:T(2,128)(2,1)S(1)}, u32[]{:S(2)}, u32[]{:S(2)}) %all-to-all-start.11) | async-done | bytes 786464 | tf_op jit(solution)/shard_map/all_to_all | solution.py:71
  514.1 4.9 collective-permute-done.5
  520.3 11.8 %scatter_fusion.6 = bf16[16,12,2048]{2,0,1:T(8,128)(2,1)S(1)} fusion(bf16[16,12,2048]{2,0,1:T(8,128)(2,1)S(1)} %broadcast.475, s32[128]{0:T(128)S(1)} %get-tuple-element.14, bf16[128,2048]{1,0:T(8,128)(2,1)S(1)} %gather_fusion.12), kind=kCustom, calls=%fused_computation.20 | custom fusion | bytes 1573888 | tf_op jit(solution)/shard_map/scatter | solution.py:63
  533.3 23.4 %all_to_all.76 = bf16[8,2,12,2048]{3,1,2,0:T(2,128)(2,1)S(1)} all-to-all(bf16[8,2,12,2048]{3,1,2,0:T(2,128)(2,1)S(1)} %copy.115), channel_id=1, replica_groups=mesh['section'=4,'expert'=8] {'expert'}, dimensions={0} | all-to-all | bytes 1572864 | tf_op jit(solution)/shard_map/all_to_all | solution.py:65
  560.6 6.8 %fusion.63 = bf16[8,2,12,2048]{3,2,0,1:T(8,128)(2,1)S(1)} fusion(bf16[1,2,768,2048]{3,2,1,0:T(8,128)(2,1)} %param.11, bf16[1,2,2048,768]{3,2,1,0:T(8,128)(2,1)} %param.10, bf16[8,2,12,2048]{3,1,2,0:T(2,128)(2,1)S(1)} %all_to_all.76, f32[8,2,12,768]{3,2,0,1:T(8,128)S(1)} %fusion.102), kind=kOutput, calls=%fused_computation.70 | convolution fusion | flops 1209237504 | bytes 14745600 | tf_op jit(solution)/shard_map/nesf,efd->nesd/dot_general | solution.py:72
  573.5 20.1 %all-to-all-done.13 = bf16[8,2,12,2048]{3,1,2,0:T(2,128)(2,1)S(1)} async-done(((bf16[8,2,12,2048]{3,1,2,0:T(2,128)(2,1)}), bf16[8,2,12,2048]{3,1,2,0:T(2,128)(2,1)S(1)}, u32[]{:S(2)}, u32[]{:S(2)}) %all-to-all-start.13) | async-done | bytes 786464 | tf_op jit(solution)/shard_map/all_to_all | solution.py:71
  (180 shorter events, 139.9 us)
Async XLA Ops:
  47.8 12.0 %copy-start.2 = (f32[1,4,16,8]{2,3,1,0:T(8,128)S(1)}, f32[1,4,16,8]{2,3,1,0:T(8,128)}, u32[]{:S(2)}) copy-start(f32[1,4,16,8]{2,3,1,0:T(8,128)} %param.13) | copy-start | bytes 6148
  54.5 30.0 %copy-start = (bf16[4,16,2048]{2,1,0:T(8,128)(2,1)S(1)}, bf16[4,16,2048]{2,1,0:T(8,128)(2,1)}, u32[]{:S(2)}) copy-start(bf16[4,16,2048]{2,1,0:T(8,128)(2,1)} %param.7) | copy-start | bytes 786436
  54.5 37.3 %copy-start.1 = (f32[1,2048]{1,0:T(1,128)S(1)}, f32[1,2048]{1,0:T(1,128)}, u32[]{:S(2)}) copy-start(f32[1,2048]{1,0:T(1,128)} %param.8) | copy-start | bytes 24580
  56.2 24.4 %all-to-all-start.1 = ((bf16[8,2,12,2048]{3,1,2,0:T(2,128)(2,1)}), bf16[8,2,12,2048]{3,1,2,0:T(2,128)(2,1)S(1)}, u32[]{:S(2)}, u32[]{:S(2)}) async-start(bf16[8,2,12,2048]{3,1,2,0:T(2,128)(2,1)} %copy.70), calls=%async_computation.1 | async-start | bytes 1572864 | tf_op jit(solution)/shard_map/all_to_all | solution.py:71
  84.6 7.1 %collective-permute-start = (bf16[16,2048]{1,0:T(8,128)(2,1)S(1)}, bf16[16,2048]{1,0:T(8,128)(2,1)S(1)}, u32[]{:S(2)}, u32[]{:S(2)}) collective-permute-start(bf16[16,2048]{1,0:T(8,128)(2,1)S(1)} %fusion.288), channel_id=1, source_target_pairs={{0,8},{8,16},{16,24},{1,9},{9,17},{17,25},{2,10},{10,18},{18,26},{... | collective-permute-start | bytes 196616 | tf_op jit(solution)/shard_map/ppermute | solution.py:13
  141.7 24.4 %all-to-all-start.3 = ((bf16[8,2,12,2048]{3,1,2,0:T(2,128)(2,1)}), bf16[8,2,12,2048]{3,1,2,0:T(2,128)(2,1)S(1)}, u32[]{:S(2)}, u32[]{:S(2)}) async-start(bf16[8,2,12,2048]{3,1,2,0:T(2,128)(2,1)} %copy.78), calls=%async_computation.3 | async-start | bytes 1572864 | tf_op jit(solution)/shard_map/all_to_all | solution.py:71
  170.0 7.1 %collective-permute-start.1 = (bf16[16,2048]{1,0:T(8,128)(2,1)S(1)}, bf16[16,2048]{1,0:T(8,128)(2,1)S(1)}, u32[]{:S(2)}, u32[]{:S(2)}) collective-permute-start(bf16[16,2048]{1,0:T(8,128)(2,1)S(1)} %get-tuple-element.41), channel_id=1, source_target_pairs={{0,8},{8,16},{16,24},{1,9},{9,17},{17,25},{2,10},{10,18},{18,26},{... | collective-permute-start | bytes 196616 | tf_op jit(solution)/shard_map/ppermute | solution.py:13
  227.1 24.4 %all-to-all-start.5 = ((bf16[8,2,12,2048]{3,1,2,0:T(2,128)(2,1)}), bf16[8,2,12,2048]{3,1,2,0:T(2,128)(2,1)S(1)}, u32[]{:S(2)}, u32[]{:S(2)}) async-start(bf16[8,2,12,2048]{3,1,2,0:T(2,128)(2,1)} %copy.86), calls=%async_computation.5 | async-start | bytes 1572864 | tf_op jit(solution)/shard_map/all_to_all | solution.py:71
  255.5 7.1 %collective-permute-start.2 = (bf16[16,2048]{1,0:T(8,128)(2,1)S(1)}, bf16[16,2048]{1,0:T(8,128)(2,1)S(1)}, u32[]{:S(2)}, u32[]{:S(2)}) collective-permute-start(bf16[16,2048]{1,0:T(8,128)(2,1)S(1)} %get-tuple-element.35), channel_id=1, source_target_pairs={{0,8},{8,16},{16,24},{1,9},{9,17},{17,25},{2,10},{10,18},{18,26},{... | collective-permute-start | bytes 196616 | tf_op jit(solution)/shard_map/ppermute | solution.py:13
  312.6 24.4 %all-to-all-start.7 = ((bf16[8,2,12,2048]{3,1,2,0:T(2,128)(2,1)}), bf16[8,2,12,2048]{3,1,2,0:T(2,128)(2,1)S(1)}, u32[]{:S(2)}, u32[]{:S(2)}) async-start(bf16[8,2,12,2048]{3,1,2,0:T(2,128)(2,1)} %copy.94), calls=%async_computation.7 | async-start | bytes 1572864 | tf_op jit(solution)/shard_map/all_to_all | solution.py:71
  341.0 7.1 %collective-permute-start.3 = (bf16[16,2048]{1,0:T(8,128)(2,1)S(1)}, bf16[16,2048]{1,0:T(8,128)(2,1)S(1)}, u32[]{:S(2)}, u32[]{:S(2)}) collective-permute-start(bf16[16,2048]{1,0:T(8,128)(2,1)S(1)} %get-tuple-element.29), channel_id=1, source_target_pairs={{0,8},{8,16},{16,24},{1,9},{9,17},{17,25},{2,10},{10,18},{18,26},{... | collective-permute-start | bytes 196616 | tf_op jit(solution)/shard_map/ppermute | solution.py:13
  398.1 24.4 %all-to-all-start.9 = ((bf16[8,2,12,2048]{3,1,2,0:T(2,128)(2,1)}), bf16[8,2,12,2048]{3,1,2,0:T(2,128)(2,1)S(1)}, u32[]{:S(2)}, u32[]{:S(2)}) async-start(bf16[8,2,12,2048]{3,1,2,0:T(2,128)(2,1)} %copy.102), calls=%async_computation.9 | async-start | bytes 1572864 | tf_op jit(solution)/shard_map/all_to_all | solution.py:71
  426.4 7.1 %collective-permute-start.4 = (bf16[16,2048]{1,0:T(8,128)(2,1)S(1)}, bf16[16,2048]{1,0:T(8,128)(2,1)S(1)}, u32[]{:S(2)}, u32[]{:S(2)}) collective-permute-start(bf16[16,2048]{1,0:T(8,128)(2,1)S(1)} %get-tuple-element.23), channel_id=1, source_target_pairs={{0,8},{8,16},{16,24},{1,9},{9,17},{17,25},{2,10},{10,18},{18,26},{... | collective-permute-start | bytes 196616 | tf_op jit(solution)/shard_map/ppermute | solution.py:13
  483.6 24.4 %all-to-all-start.11 = ((bf16[8,2,12,2048]{3,1,2,0:T(2,128)(2,1)}), bf16[8,2,12,2048]{3,1,2,0:T(2,128)(2,1)S(1)}, u32[]{:S(2)}, u32[]{:S(2)}) async-start(bf16[8,2,12,2048]{3,1,2,0:T(2,128)(2,1)} %copy.110), calls=%async_computation.11 | async-start | bytes 1572864 | tf_op jit(solution)/shard_map/all_to_all | solution.py:71
  512.0 7.1 %collective-permute-start.5 = (bf16[16,2048]{1,0:T(8,128)(2,1)S(1)}, bf16[16,2048]{1,0:T(8,128)(2,1)S(1)}, u32[]{:S(2)}, u32[]{:S(2)}) collective-permute-start(bf16[16,2048]{1,0:T(8,128)(2,1)S(1)} %get-tuple-element.17), channel_id=1, source_target_pairs={{0,8},{8,16},{16,24},{1,9},{9,17},{17,25},{2,10},{10,18},{18,26},{... | collective-permute-start | bytes 196616 | tf_op jit(solution)/shard_map/ppermute | solution.py:13
  569.1 24.4 %all-to-all-start.13 = ((bf16[8,2,12,2048]{3,1,2,0:T(2,128)(2,1)}), bf16[8,2,12,2048]{3,1,2,0:T(2,128)(2,1)S(1)}, u32[]{:S(2)}, u32[]{:S(2)}) async-start(bf16[8,2,12,2048]{3,1,2,0:T(2,128)(2,1)} %copy.118), calls=%async_computation.13 | async-start | bytes 1572864 | tf_op jit(solution)/shard_map/all_to_all | solution.py:71
where the time goes:
time: 608 us; the launch traced here: 598 us
  waiting for transfers between devices  168 us (28%)
  blocking collectives  166 us (27%)
  local copies, waits for them, and re-layouts  137 us (23%)
  matrix products  75 us (12%)
  starting transfers between devices  40.1 us (7%)
  other arithmetic  10.5 us (2%)
    all_to_all x7, blocking collectives, on_device(): lax.all_to_all(outgoing, 'expert', split_axis=0, concat_axis=0, tiled=True)  166 us
    all_to_all x7, waiting for transfers between devices, on_device(): lax.all_to_all(jnp.einsum('nesf,efd->nesd', inner, w_down, preferred_elem...  141 us
    scatter x7, local copies, waits for them, and re-layouts, on_device(): outgoing = outgoing.at[flat_ids, slot_index].set(normed[token_index])  82.9 us
    dot_general x7, matrix products, on_device(): jnp.einsum('nesf,efd->nesd', inner, w_down, preferred_element_type=jnp.fl...  47.4 us
    dot_general x7, matrix products, on_device(): jnp.einsum('nesd,edf->nesf', received, w_gate, preferred_element_type=jnp...  27.6 us
    ppermute x6, waiting for transfers between devices, shifted(): return lax.ppermute(array, axis, pairs)  27 us
    all_to_all x7, starting transfers between devices, on_device(): lax.all_to_all(jnp.einsum('nesf,efd->nesd', inner, w_down, preferred_elem...  24.8 us
    gather x7, local copies, waits for them, and re-layouts, on_device(): picked = returned[flat_ids, slot_index].reshape(tok_rows, topk, width)  17 us
  transfers between devices with their start and end apart: 13, of which 13 were waited for; matrix products, arithmetic and copies ran while one was open for 1% of the time, Pallas kernels for 0%

commit v1 on v0

--- a/solution.py
+++ b/solution.py
@@ -5,6 +5,22 @@
 
 MB = 4
 EPSILON = 1e-06
+
+
+def exchange_in_pairs(x, axis, split, join):
+    ways, here = (lax.axis_size(axis), lax.axis_index(axis))
+    width = x.shape[split] // ways
+    dims = list(x.shape)
+    dims[split] = width
+    height = dims[join]
+    dims[join] = height * ways
+    full = jnp.zeros(dims, x.dtype)
+    for mask in range(ways):
+        part = lax.dynamic_slice_in_dim(x, (here ^ mask) * width, width, axis=split)
+        if mask:
+            part = lax.ppermute(part, axis, [(d, d ^ mask) for d in range(ways)])
+        full = lax.dynamic_update_slice_in_dim(full, part, (here ^ mask) * height, axis=join)
+    return full
 
 
 def shifted(array, axis, by):
@@ -68,14 +84,13 @@
         )
         up_part = jnp.einsum("nesd,edf->nesf", received, w_up, preferred_element_type=jnp.float32)
         inner = (jax.nn.silu(gate_part) * up_part).astype(jnp.bfloat16)
-        returned = lax.all_to_all(
+        returned = exchange_in_pairs(
             jnp.einsum("nesf,efd->nesd", inner, w_down, preferred_element_type=jnp.float32).astype(
                 jnp.bfloat16
             ),
             "expert",
-            split_axis=0,
-            concat_axis=0,
-            tiled=True,
+            0,
+            0,
         )
         returned = returned.reshape(experts, capacity, width)
         picked = returned[flat_ids, slot_index].reshape(tok_rows, topk, width)

time: 608 us -> 579 us (0.952)
  blocking collectives: 166 us -> 0 us
  starting transfers between devices: 40.1 us -> 112 us
  waiting for transfers between devices: 168 us -> 231 us
    all_to_all x7 -> x0, blocking collectives: 166 us -> none  [on_device(): lax.all_to_all(outgoing, 'expert', split_axis=0, concat_axis=0, tiled=True)]
    ppermute x0 -> x49, starting transfers between devices: none -> 59.4 us  [exchange_in_pairs(): part = lax.ppermute(part, axis, [(d, d ^ mask) for d in range(ways)])]
    ppermute x0 -> x49, waiting for transfers between devices: none -> 56.7 us  [exchange_in_pairs(): part = lax.ppermute(part, axis, [(d, d ^ mask) for d in range(ways)])]
    all_to_all x7, starting transfers between devices: 24.8 us -> 39.1 us  [on_device(): lax.all_to_all(outgoing, 'expert', split_axis=0, concat_axis=0, tiled=True)]
    convert_element_type x7 -> x0, local copies, waits for them, and re-layouts: 11.8 us -> none  [on_device(): jnp.einsum('nesf,efd->nesd', inner, w_down, preferred_element_type=jnp.fl...]
    another operation x7 -> x70, local copies, waits for them, and re-layouts: 0.54 us -> 9.97 us
    reshape x14, local copies, waits for them, and re-layouts: 7.68 us -> 14 us  [on_device(): outgoing = outgoing.reshape(devices, local_experts, capacity, width)]
  transfers between devices with their start and end apart: 13 -> 62, of which waited for: 13 -> 27; matrix products, arithmetic and copies ran while one was open for 1% -> 3% of each run, Pallas kernels for 0% -> 0%
where the time goes in v1:
time: 579 us; the launch traced here: 571 us
  waiting for transfers between devices  231 us (40%)
  local copies, waits for them, and re-layouts  141 us (24%)
  starting transfers between devices  112 us (19%)
  matrix products  75.2 us (13%)
  other arithmetic  10 us (2%)
    all_to_all x7, waiting for transfers between devices, on_device(): lax.all_to_all(outgoing, 'expert', split_axis=0, concat_axis=0, tiled=True)  142 us
    scatter x7, local copies, waits for them, and re-layouts, on_device(): outgoing = outgoing.at[flat_ids, slot_index].set(normed[token_index])  82.9 us
    ppermute x49, starting transfers between devices, exchange_in_pairs(): part = lax.ppermute(part, axis, [(d, d ^ mask) for d in range(ways)])  59.4 us
    ppermute x49, waiting for transfers between devices, exchange_in_pairs(): part = lax.ppermute(part, axis, [(d, d ^ mask) for d in range(ways)])  56.7 us
    dot_general x7, matrix products, on_device(): jnp.einsum('nesf,efd->nesd', inner, w_down, preferred_element_type=jnp.fl...  47.5 us
    all_to_all x7, starting transfers between devices, on_device(): lax.all_to_all(outgoing, 'expert', split_axis=0, concat_axis=0, tiled=True)  39.1 us
    ppermute x6, waiting for transfers between devices, shifted(): return lax.ppermute(array, axis, pairs)  32.3 us
    dot_general x7, matrix products, on_device(): jnp.einsum('nesd,edf->nesf', received, w_gate, preferred_element_type=jnp...  27.7 us
  transfers between devices with their start and end apart: 62, of which 27 were waited for; matrix products, arithmetic and copies ran while one was open for 3% of the time, Pallas kernels for 0%

profile of v1, /device:TPU:4, one launch (start us, length us, event | category | flops | bytes accessed | tf_op | source)
XLA Modules:
  0.0 571.4 jit_solution(6535417229599122050)
XLA Ops:
  4.5 11.8 %scatter_fusion = bf16[16,12,2048]{2,0,1:T(8,128)(2,1)S(1)} fusion(bf16[16,12,2048]{2,0,1:T(8,128)(2,1)S(1)} %broadcast.479.clone, s32[128]{0:T(128)S(1)} %get-tuple-element.46, bf16[128,2048]{1,0:T(8,128)(2,1)S(1)} %gather_fusion), kind=kCustom, calls=%fused_computation.14 | custom fusion | bytes 1573888 | tf_op jit(solution)/shard_map/scatter | solution.py:79
  25.2 19.6 %all-to-all-done = bf16[8,2,12,2048]{3,1,2,0:T(2,128)(2,1)S(1)} async-done(((bf16[8,2,12,2048]{3,1,2,0:T(2,128)(2,1)}), bf16[8,2,12,2048]{3,1,2,0:T(2,128)(2,1)S(1)}, u32[]{:S(2)}, u32[]{:S(2)}) %all-to-all-start) | async-done | bytes 786464 | tf_op jit(solution)/shard_map/all_to_all | solution.py:81
  48.7 6.8 %fusion.42 = bf16[2,8,12,2048]{3,2,1,0:T(8,128)(2,1)S(1)} fusion(bf16[1,2,768,2048]{3,2,1,0:T(8,128)(2,1)} %param.11, bf16[1,2,2048,768]{3,2,1,0:T(8,128)(2,1)} %param.10, bf16[8,2,12,2048]{3,1,2,0:T(2,128)(2,1)S(1)} %all-to-all-done, f32[8,2,12,768]{3,2,0,1:T(8,128)S(1)} %fusion.63), kind=kOutput, calls=%fused_computation.63 | convolution fusion | flops 1209237504 | bytes 14745600 | tf_op jit(solution)/shard_map/nesf,efd->nesd/dot_general | solution.py:88
  65.9 7.3 %collective-permute-done.3 = bf16[1,2,12,2048]{3,1,2,0:T(2,128)(2,1)S(1)} collective-permute-done((bf16[1,2,12,2048]{3,1,2,0:T(2,128)(2,1)S(1)}, bf16[1,2,12,2048]{3,1,2,0:T(2,128)(2,1)S(1)}, u32[]{:S(2)}, u32[]{:S(2)}) %collective-permute-start.3) | collective-permute-done | bytes 98336 | tf_op jit(solution)/shard_map/ppermute | solution.py:21
  86.5 11.8 %scatter_fusion.1 = bf16[16,12,2048]{2,0,1:T(8,128)(2,1)S(1)} fusion(bf16[16,12,2048]{2,0,1:T(8,128)(2,1)S(1)} %broadcast.479.clone.1, s32[128]{0:T(128)S(1)} %get-tuple-element.44, bf16[128,2048]{1,0:T(8,128)(2,1)S(1)} %gather_fusion.2), kind=kCustom, calls=%fused_computation.15 | custom fusion | bytes 1573888 | tf_op jit(solution)/shard_map/scatter | solution.py:79
  106.0 20.8 %all-to-all-done.1 = bf16[8,2,12,2048]{3,1,2,0:T(2,128)(2,1)S(1)} async-done(((bf16[8,2,12,2048]{3,1,2,0:T(2,128)(2,1)}), bf16[8,2,12,2048]{3,1,2,0:T(2,128)(2,1)S(1)}, u32[]{:S(2)}, u32[]{:S(2)}) %all-to-all-start.1) | async-done | bytes 786464 | tf_op jit(solution)/shard_map/all_to_all | solution.py:81
  130.7 6.8 %fusion.45 = bf16[2,8,12,2048]{3,2,1,0:T(8,128)(2,1)S(1)} fusion(bf16[1,2,768,2048]{3,2,1,0:T(8,128)(2,1)} %param.11, bf16[1,2,2048,768]{3,2,1,0:T(8,128)(2,1)} %param.10, bf16[8,2,12,2048]{3,1,2,0:T(2,128)(2,1)S(1)} %all-to-all-done.1, f32[8,2,12,768]{3,2,0,1:T(8,128)S(1)} %fusion.66), kind=kOutput, calls=%fused_computation.64 | convolution fusion | flops 1209237504 | bytes 14745600 | tf_op jit(solution)/shard_map/nesf,efd->nesd/dot_general | solution.py:88
  147.8 7.3 %collective-permute-done.11 = bf16[1,2,12,2048]{3,1,2,0:T(2,128)(2,1)S(1)} collective-permute-done((bf16[1,2,12,2048]{3,1,2,0:T(2,128)(2,1)S(1)}, bf16[1,2,12,2048]{3,1,2,0:T(2,128)(2,1)S(1)}, u32[]{:S(2)}, u32[]{:S(2)}) %collective-permute-start.11) | collective-permute-done | bytes 98336 | tf_op jit(solution)/shard_map/ppermute | solution.py:21
  168.5 11.8 %scatter_fusion.2 = bf16[16,12,2048]{2,0,1:T(8,128)(2,1)S(1)} fusion(bf16[16,12,2048]{2,0,1:T(8,128)(2,1)S(1)} %broadcast.479.clone.2, s32[128]{0:T(128)S(1)} %get-tuple-element.38, bf16[128,2048]{1,0:T(8,128)(2,1)S(1)} %gather_fusion.4), kind=kCustom, calls=%fused_computation.16 | custom fusion | bytes 1573888 | tf_op jit(solution)/shard_map/scatter | solution.py:79
  182.4 5.8 %all-to-all-start.2 = ((bf16[8,2,12,2048]{3,1,2,0:T(2,128)(2,1)}), bf16[8,2,12,2048]{3,1,2,0:T(2,128)(2,1)S(1)}, u32[]{:S(2)}, u32[]{:S(2)}) async-start(bf16[8,2,12,2048]{3,1,2,0:T(2,128)(2,1)} %copy.216), calls=%async_computation.2 | async-start | bytes 1572864 | tf_op jit(solution)/shard_map/all_to_all | solution.py:81
  189.4 19.7 %all-to-all-done.2 = bf16[8,2,12,2048]{3,1,2,0:T(2,128)(2,1)S(1)} async-done(((bf16[8,2,12,2048]{3,1,2,0:T(2,128)(2,1)}), bf16[8,2,12,2048]{3,1,2,0:T(2,128)(2,1)S(1)}, u32[]{:S(2)}, u32[]{:S(2)}) %all-to-all-start.2) | async-done | bytes 786464 | tf_op jit(solution)/shard_map/all_to_all | solution.py:81
  213.1 6.8 %fusion.48 = bf16[2,8,12,2048]{3,2,1,0:T(8,128)(2,1)S(1)} fusion(bf16[1,2,768,2048]{3,2,1,0:T(8,128)(2,1)} %param.11, bf16[1,2,2048,768]{3,2,1,0:T(8,128)(2,1)} %param.10, bf16[8,2,12,2048]{3,1,2,0:T(2,128)(2,1)S(1)} %all-to-all-done.2, f32[8,2,12,768]{3,2,0,1:T(8,128)S(1)} %fusion.69), kind=kOutput, calls=%fused_computation.65 | convolution fusion | flops 1209237504 | bytes 14745600 | tf_op jit(solution)/shard_map/nesf,efd->nesd/dot_general | solution.py:88
  230.2 7.2 %collective-permute-done.19 = bf16[1,2,12,2048]{3,1,2,0:T(2,128)(2,1)S(1)} collective-permute-done((bf16[1,2,12,2048]{3,1,2,0:T(2,128)(2,1)S(1)}, bf16[1,2,12,2048]{3,1,2,0:T(2,128)(2,1)S(1)}, u32[]{:S(2)}, u32[]{:S(2)}) %collective-permute-start.19) | collective-permute-done | bytes 98336 | tf_op jit(solution)/shard_map/ppermute | solution.py:21
  243.8 5.8 %collective-permute-done.23 = bf16[16,2048]{1,0:T(8,128)(2,1)S(1)} collective-permute-done((bf16[16,2048]{1,0:T(8,128)(2,1)S(1)}, bf16[16,2048]{1,0:T(8,128)(2,1)S(1)}, u32[]{:S(2)}, u32[]{:S(2)}) %collective-permute-start.23) | collective-permute-done | bytes 65568 | tf_op jit(solution)/shard_map/ppermute | solution.py:29
  250.9 11.8 %scatter_fusion.3 = bf16[16,12,2048]{2,0,1:T(8,128)(2,1)S(1)} fusion(bf16[16,12,2048]{2,0,1:T(8,128)(2,1)S(1)} %broadcast.479.clone.3, s32[128]{0:T(128)S(1)} %get-tuple-element.32, bf16[128,2048]{1,0:T(8,128)(2,1)S(1)} %gather_fusion.6), kind=kCustom, calls=%fused_computation.17 | custom fusion | bytes 1573888 | tf_op jit(solution)/shard_map/scatter | solution.py:79
  270.4 20.8 %all-to-all-done.3 = bf16[8,2,12,2048]{3,1,2,0:T(2,128)(2,1)S(1)} async-done(((bf16[8,2,12,2048]{3,1,2,0:T(2,128)(2,1)}), bf16[8,2,12,2048]{3,1,2,0:T(2,128)(2,1)S(1)}, u32[]{:S(2)}, u32[]{:S(2)}) %all-to-all-start.3) | async-done | bytes 786464 | tf_op jit(solution)/shard_map/all_to_all | solution.py:81
  295.2 6.8 %fusion.51 = bf16[2,8,12,2048]{3,2,1,0:T(8,128)(2,1)S(1)} fusion(bf16[1,2,768,2048]{3,2,1,0:T(8,128)(2,1)} %param.11, bf16[1,2,2048,768]{3,2,1,0:T(8,128)(2,1)} %param.10, bf16[8,2,12,2048]{3,1,2,0:T(2,128)(2,1)S(1)} %all-to-all-done.3, f32[8,2,12,768]{3,2,0,1:T(8,128)S(1)} %fusion.72), kind=kOutput, calls=%fused_computation.66 | convolution fusion | flops 1209237504 | bytes 14745600 | tf_op jit(solution)/shard_map/nesf,efd->nesd/dot_general | solution.py:88
  312.3 7.2 %collective-permute-done.27 = bf16[1,2,12,2048]{3,1,2,0:T(2,128)(2,1)S(1)} collective-permute-done((bf16[1,2,12,2048]{3,1,2,0:T(2,128)(2,1)S(1)}, bf16[1,2,12,2048]{3,1,2,0:T(2,128)(2,1)S(1)}, u32[]{:S(2)}, u32[]{:S(2)}) %collective-permute-start.27) | collective-permute-done | bytes 98336 | tf_op jit(solution)/shard_map/ppermute | solution.py:21
  325.9 5.8 %collective-permute-done.31 = bf16[16,2048]{1,0:T(8,128)(2,1)S(1)} collective-permute-done((bf16[16,2048]{1,0:T(8,128)(2,1)S(1)}, bf16[16,2048]{1,0:T(8,128)(2,1)S(1)}, u32[]{:S(2)}, u32[]{:S(2)}) %collective-permute-start.31) | collective-permute-done | bytes 65568 | tf_op jit(solution)/shard_map/ppermute | solution.py:29
  333.0 11.9 %scatter_fusion.4 = bf16[16,12,2048]{2,0,1:T(8,128)(2,1)S(1)} fusion(bf16[16,12,2048]{2,0,1:T(8,128)(2,1)S(1)} %broadcast.479.clone.4, s32[128]{0:T(128)S(1)} %get-tuple-element.26, bf16[128,2048]{1,0:T(8,128)(2,1)S(1)} %gather_fusion.8), kind=kCustom, calls=%fused_computation.18 | custom fusion | bytes 1573888 | tf_op jit(solution)/shard_map/scatter | solution.py:79
  353.7 19.7 %all-to-all-done.4 = bf16[8,2,12,2048]{3,1,2,0:T(2,128)(2,1)S(1)} async-done(((bf16[8,2,12,2048]{3,1,2,0:T(2,128)(2,1)}), bf16[8,2,12,2048]{3,1,2,0:T(2,128)(2,1)S(1)}, u32[]{:S(2)}, u32[]{:S(2)}) %all-to-all-start.4) | async-done | bytes 786464 | tf_op jit(solution)/shard_map/all_to_all | solution.py:81
  377.4 6.8 %fusion.54 = bf16[2,8,12,2048]{3,2,1,0:T(8,128)(2,1)S(1)} fusion(bf16[1,2,768,2048]{3,2,1,0:T(8,128)(2,1)} %param.11, bf16[1,2,2048,768]{3,2,1,0:T(8,128)(2,1)} %param.10, bf16[8,2,12,2048]{3,1,2,0:T(2,128)(2,1)S(1)} %all-to-all-done.4, f32[8,2,12,768]{3,2,0,1:T(8,128)S(1)} %fusion.75), kind=kOutput, calls=%fused_computation.67 | convolution fusion | flops 1209237504 | bytes 14745600 | tf_op jit(solution)/shard_map/nesf,efd->nesd/dot_general | solution.py:88
  394.5 7.3 %collective-permute-done.35 = bf16[1,2,12,2048]{3,1,2,0:T(2,128)(2,1)S(1)} collective-permute-done((bf16[1,2,12,2048]{3,1,2,0:T(2,128)(2,1)S(1)}, bf16[1,2,12,2048]{3,1,2,0:T(2,128)(2,1)S(1)}, u32[]{:S(2)}, u32[]{:S(2)}) %collective-permute-start.35) | collective-permute-done | bytes 98336 | tf_op jit(solution)/shard_map/ppermute | solution.py:21
  415.1 11.8 %scatter_fusion.5 = bf16[16,12,2048]{2,0,1:T(8,128)(2,1)S(1)} fusion(bf16[16,12,2048]{2,0,1:T(8,128)(2,1)S(1)} %broadcast.479.clone.5, s32[128]{0:T(128)S(1)} %get-tuple-element.20, bf16[128,2048]{1,0:T(8,128)(2,1)S(1)} %gather_fusion.10), kind=kCustom, calls=%fused_computation.19 | custom fusion | bytes 1573888 | tf_op jit(solution)/shard_map/scatter | solution.py:79
  434.9 20.8 %all-to-all-done.5 = bf16[8,2,12,2048]{3,1,2,0:T(2,128)(2,1)S(1)} async-done(((bf16[8,2,12,2048]{3,1,2,0:T(2,128)(2,1)}), bf16[8,2,12,2048]{3,1,2,0:T(2,128)(2,1)S(1)}, u32[]{:S(2)}, u32[]{:S(2)}) %all-to-all-start.5) | async-done | bytes 786464 | tf_op jit(solution)/shard_map/all_to_all | solution.py:81
  459.7 6.8 %fusion.57 = bf16[2,8,12,2048]{3,2,1,0:T(8,128)(2,1)S(1)} fusion(bf16[1,2,768,2048]{3,2,1,0:T(8,128)(2,1)} %param.11, bf16[1,2,2048,768]{3,2,1,0:T(8,128)(2,1)} %param.10, bf16[8,2,12,2048]{3,1,2,0:T(2,128)(2,1)S(1)} %all-to-all-done.5, f32[8,2,12,768]{3,2,0,1:T(8,128)S(1)} %fusion.78), kind=kOutput, calls=%fused_computation.68 | convolution fusion | flops 1209237504 | bytes 14745600 | tf_op jit(solution)/shard_map/nesf,efd->nesd/dot_general | solution.py:88
  476.8 7.2 %collective-permute-done.43 = bf16[1,2,12,2048]{3,1,2,0:T(2,128)(2,1)S(1)} collective-permute-done((bf16[1,2,12,2048]{3,1,2,0:T(2,128)(2,1)S(1)}, bf16[1,2,12,2048]{3,1,2,0:T(2,128)(2,1)S(1)}, u32[]{:S(2)}, u32[]{:S(2)}) %collective-permute-start.43) | collective-permute-done | bytes 98336 | tf_op jit(solution)/shard_map/ppermute | solution.py:21
  490.4 5.8 %collective-permute-done.47 = bf16[16,2048]{1,0:T(8,128)(2,1)S(1)} collective-permute-done((bf16[16,2048]{1,0:T(8,128)(2,1)S(1)}, bf16[16,2048]{1,0:T(8,128)(2,1)S(1)}, u32[]{:S(2)}, u32[]{:S(2)}) %collective-permute-start.47) | collective-permute-done | bytes 65568 | tf_op jit(solution)/shard_map/ppermute | solution.py:29
  497.5 11.8 %scatter_fusion.6 = bf16[16,12,2048]{2,0,1:T(8,128)(2,1)S(1)} fusion(bf16[16,12,2048]{2,0,1:T(8,128)(2,1)S(1)} %broadcast.479, s32[128]{0:T(128)S(1)} %get-tuple-element.14, bf16[128,2048]{1,0:T(8,128)(2,1)S(1)} %gather_fusion.12), kind=kCustom, calls=%fused_computation.20 | custom fusion | bytes 1573888 | tf_op jit(solution)/shard_map/scatter | solution.py:79
  517.7 20.2 %all-to-all-done.6 = bf16[8,2,12,2048]{3,1,2,0:T(2,128)(2,1)S(1)} async-done(((bf16[8,2,12,2048]{3,1,2,0:T(2,128)(2,1)}), bf16[8,2,12,2048]{3,1,2,0:T(2,128)(2,1)S(1)}, u32[]{:S(2)}, u32[]{:S(2)}) %all-to-all-start.6) | async-done | bytes 786464 | tf_op jit(solution)/shard_map/all_to_all | solution.py:81
  541.8 6.8 %fusion.60 = bf16[2,8,12,2048]{3,2,1,0:T(8,128)(2,1)S(1)} fusion(bf16[1,2,768,2048]{3,2,1,0:T(8,128)(2,1)} %param.11, bf16[1,2,2048,768]{3,2,1,0:T(8,128)(2,1)} %param.10, bf16[8,2,12,2048]{3,1,2,0:T(2,128)(2,1)S(1)} %all-to-all-done.6, f32[8,2,12,768]{3,2,0,1:T(8,128)S(1)} %fusion.81), kind=kOutput, calls=%fused_computation.69 | convolution fusion | flops 1209237504 | bytes 14745600 | tf_op jit(solution)/shard_map/nesf,efd->nesd/dot_general | solution.py:88
  558.9 7.2 %collective-permute-done.51 = bf16[1,2,12,2048]{3,1,2,0:T(2,128)(2,1)S(1)} collective-permute-done((bf16[1,2,12,2048]{3,1,2,0:T(2,128)(2,1)S(1)}, bf16[1,2,12,2048]{3,1,2,0:T(2,128)(2,1)S(1)}, u32[]{:S(2)}, u32[]{:S(2)}) %collective-permute-start.51) | collective-permute-done | bytes 98336 | tf_op jit(solution)/shard_map/ppermute | solution.py:21
  (376 shorter events, 223.2 us)
Async XLA Ops:
  18.4 26.4 %all-to-all-start = ((bf16[8,2,12,2048]{3,1,2,0:T(2,128)(2,1)}), bf16[8,2,12,2048]{3,1,2,0:T(2,128)(2,1)S(1)}, u32[]{:S(2)}, u32[]{:S(2)}) async-start(bf16[8,2,12,2048]{3,1,2,0:T(2,128)(2,1)} %copy.172), calls=%async_computation | async-start | bytes 1572864 | tf_op jit(solution)/shard_map/all_to_all | solution.py:81
  58.1 15.0 %collective-permute-start.3 = (bf16[1,2,12,2048]{3,1,2,0:T(2,128)(2,1)S(1)}, bf16[1,2,12,2048]{3,1,2,0:T(2,128)(2,1)S(1)}, u32[]{:S(2)}, u32[]{:S(2)}) collective-permute-start(bf16[1,2,12,2048]{3,1,2,0:T(2,128)(2,1)S(1)} %bitcast.728), channel_id=1, source_target_pairs={{0,4},{1,5},{2,6},{3,7},{4,0},{5,1},{6,2},{7,3},{8,12},{9,13},{10,... | collective-permute-start | bytes 294920 | tf_op jit(solution)/shard_map/ppermute | solution.py:21
  58.4 15.6 %collective-permute-start.4 = (bf16[1,2,12,2048]{3,1,2,0:T(2,128)(2,1)S(1)}, bf16[1,2,12,2048]{3,1,2,0:T(2,128)(2,1)S(1)}, u32[]{:S(2)}, u32[]{:S(2)}) collective-permute-start(bf16[1,2,12,2048]{3,1,2,0:T(2,128)(2,1)S(1)} %bitcast.722), channel_id=1, source_target_pairs={{0,5},{1,4},{2,7},{3,6},{4,1},{5,0},{6,3},{7,2},{8,13},{9,12},{10,... | collective-permute-start | bytes 294920 | tf_op jit(solution)/shard_map/ppermute | solution.py:21
  61.8 12.3 %collective-permute-start.5 = (bf16[1,2,12,2048]{3,1,2,0:T(2,128)(2,1)S(1)}, bf16[1,2,12,2048]{3,1,2,0:T(2,128)(2,1)S(1)}, u32[]{:S(2)}, u32[]{:S(2)}) collective-permute-start(bf16[1,2,12,2048]{3,1,2,0:T(2,128)(2,1)S(1)} %bitcast.740), channel_id=1, source_target_pairs={{0,6},{1,7},{2,4},{3,5},{4,2},{5,3},{6,0},{7,1},{8,14},{9,15},{10,... | collective-permute-start | bytes 294920 | tf_op jit(solution)/shard_map/ppermute | solution.py:21
  100.3 26.4 %all-to-all-start.1 = ((bf16[8,2,12,2048]{3,1,2,0:T(2,128)(2,1)}), bf16[8,2,12,2048]{3,1,2,0:T(2,128)(2,1)S(1)}, u32[]{:S(2)}, u32[]{:S(2)}) async-start(bf16[8,2,12,2048]{3,1,2,0:T(2,128)(2,1)} %copy.194), calls=%async_computation.1 | async-start | bytes 1572864 | tf_op jit(solution)/shard_map/all_to_all | solution.py:81
  140.1 15.0 %collective-permute-start.11 = (bf16[1,2,12,2048]{3,1,2,0:T(2,128)(2,1)S(1)}, bf16[1,2,12,2048]{3,1,2,0:T(2,128)(2,1)S(1)}, u32[]{:S(2)}, u32[]{:S(2)}) collective-permute-start(bf16[1,2,12,2048]{3,1,2,0:T(2,128)(2,1)S(1)} %bitcast.729), channel_id=1, source_target_pairs={{0,4},{1,5},{2,6},{3,7},{4,0},{5,1},{6,2},{7,3},{8,12},{9,13},{10,... | collective-permute-start | bytes 294920 | tf_op jit(solution)/shard_map/ppermute | solution.py:21
  140.3 15.6 %collective-permute-start.12 = (bf16[1,2,12,2048]{3,1,2,0:T(2,128)(2,1)S(1)}, bf16[1,2,12,2048]{3,1,2,0:T(2,128)(2,1)S(1)}, u32[]{:S(2)}, u32[]{:S(2)}) collective-permute-start(bf16[1,2,12,2048]{3,1,2,0:T(2,128)(2,1)S(1)} %bitcast.723), channel_id=1, source_target_pairs={{0,5},{1,4},{2,7},{3,6},{4,1},{5,0},{6,3},{7,2},{8,13},{9,12},{10,... | collective-permute-start | bytes 294920 | tf_op jit(solution)/shard_map/ppermute | solution.py:21
  143.8 12.3 %collective-permute-start.13 = (bf16[1,2,12,2048]{3,1,2,0:T(2,128)(2,1)S(1)}, bf16[1,2,12,2048]{3,1,2,0:T(2,128)(2,1)S(1)}, u32[]{:S(2)}, u32[]{:S(2)}) collective-permute-start(bf16[1,2,12,2048]{3,1,2,0:T(2,128)(2,1)S(1)} %bitcast.741), channel_id=1, source_target_pairs={{0,6},{1,7},{2,4},{3,5},{4,2},{5,3},{6,0},{7,1},{8,14},{9,15},{10,... | collective-permute-start | bytes 294920 | tf_op jit(solution)/shard_map/ppermute | solution.py:21
  182.4 26.7 %all-to-all-start.2 = ((bf16[8,2,12,2048]{3,1,2,0:T(2,128)(2,1)}), bf16[8,2,12,2048]{3,1,2,0:T(2,128)(2,1)S(1)}, u32[]{:S(2)}, u32[]{:S(2)}) async-start(bf16[8,2,12,2048]{3,1,2,0:T(2,128)(2,1)} %copy.216), calls=%async_computation.2 | async-start | bytes 1572864 | tf_op jit(solution)/shard_map/all_to_all | solution.py:81
  222.5 15.0 %collective-permute-start.19 = (bf16[1,2,12,2048]{3,1,2,0:T(2,128)(2,1)S(1)}, bf16[1,2,12,2048]{3,1,2,0:T(2,128)(2,1)S(1)}, u32[]{:S(2)}, u32[]{:S(2)}) collective-permute-start(bf16[1,2,12,2048]{3,1,2,0:T(2,128)(2,1)S(1)} %bitcast.730), channel_id=1, source_target_pairs={{0,4},{1,5},{2,6},{3,7},{4,0},{5,1},{6,2},{7,3},{8,12},{9,13},{10,... | collective-permute-start | bytes 294920 | tf_op jit(solution)/shard_map/ppermute | solution.py:21
  222.7 15.6 %collective-permute-start.20 = (bf16[1,2,12,2048]{3,1,2,0:T(2,128)(2,1)S(1)}, bf16[1,2,12,2048]{3,1,2,0:T(2,128)(2,1)S(1)}, u32[]{:S(2)}, u32[]{:S(2)}) collective-permute-start(bf16[1,2,12,2048]{3,1,2,0:T(2,128)(2,1)S(1)} %bitcast.724), channel_id=1, source_target_pairs={{0,5},{1,4},{2,7},{3,6},{4,1},{5,0},{6,3},{7,2},{8,13},{9,12},{10,... | collective-permute-start | bytes 294920 | tf_op jit(solution)/shard_map/ppermute | solution.py:21
  226.2 12.3 %collective-permute-start.21 = (bf16[1,2,12,2048]{3,1,2,0:T(2,128)(2,1)S(1)}, bf16[1,2,12,2048]{3,1,2,0:T(2,128)(2,1)S(1)}, u32[]{:S(2)}, u32[]{:S(2)}) collective-permute-start(bf16[1,2,12,2048]{3,1,2,0:T(2,128)(2,1)S(1)} %bitcast.742), channel_id=1, source_target_pairs={{0,6},{1,7},{2,4},{3,5},{4,2},{5,3},{6,0},{7,1},{8,14},{9,15},{10,... | collective-permute-start | bytes 294920 | tf_op jit(solution)/shard_map/ppermute | solution.py:21
  227.6 11.0 %collective-permute-start.22 = (bf16[1,2,12,2048]{3,1,2,0:T(2,128)(2,1)S(1)}, bf16[1,2,12,2048]{3,1,2,0:T(2,128)(2,1)S(1)}, u32[]{:S(2)}, u32[]{:S(2)}) collective-permute-start(bf16[1,2,12,2048]{3,1,2,0:T(2,128)(2,1)S(1)} %bitcast.718), channel_id=1, source_target_pairs={{0,7},{1,6},{2,5},{3,4},{4,3},{5,2},{6,1},{7,0},{8,15},{9,14},{10,... | collective-permute-start | bytes 294920 | tf_op jit(solution)/shard_map/ppermute | solution.py:21
  264.7 26.5 %all-to-all-start.3 = ((bf16[8,2,12,2048]{3,1,2,0:T(2,128)(2,1)}), bf16[8,2,12,2048]{3,1,2,0:T(2,128)(2,1)S(1)}, u32[]{:S(2)}, u32[]{:S(2)}) async-start(bf16[8,2,12,2048]{3,1,2,0:T(2,128)(2,1)} %copy.238), calls=%async_computation.3 | async-start | bytes 1572864 | tf_op jit(solution)/shard_map/all_to_all | solution.py:81
  304.6 15.0 %collective-permute-start.27 = (bf16[1,2,12,2048]{3,1,2,0:T(2,128)(2,1)S(1)}, bf16[1,2,12,2048]{3,1,2,0:T(2,128)(2,1)S(1)}, u32[]{:S(2)}, u32[]{:S(2)}) collective-permute-start(bf16[1,2,12,2048]{3,1,2,0:T(2,128)(2,1)S(1)} %bitcast.731), channel_id=1, source_target_pairs={{0,4},{1,5},{2,6},{3,7},{4,0},{5,1},{6,2},{7,3},{8,12},{9,13},{10,... | collective-permute-start | bytes 294920 | tf_op jit(solution)/shard_map/ppermute | solution.py:21
  304.8 15.6 %collective-permute-start.28 = (bf16[1,2,12,2048]{3,1,2,0:T(2,128)(2,1)S(1)}, bf16[1,2,12,2048]{3,1,2,0:T(2,128)(2,1)S(1)}, u32[]{:S(2)}, u32[]{:S(2)}) collective-permute-start(bf16[1,2,12,2048]{3,1,2,0:T(2,128)(2,1)S(1)} %bitcast.725), channel_id=1, source_target_pairs={{0,5},{1,4},{2,7},{3,6},{4,1},{5,0},{6,3},{7,2},{8,13},{9,12},{10,... | collective-permute-start | bytes 294920 | tf_op jit(solution)/shard_map/ppermute | solution.py:21
  308.2 12.3 %collective-permute-start.29 = (bf16[1,2,12,2048]{3,1,2,0:T(2,128)(2,1)S(1)}, bf16[1,2,12,2048]{3,1,2,0:T(2,128)(2,1)S(1)}, u32[]{:S(2)}, u32[]{:S(2)}) collective-permute-start(bf16[1,2,12,2048]{3,1,2,0:T(2,128)(2,1)S(1)} %bitcast.743), channel_id=1, source_target_pairs={{0,6},{1,7},{2,4},{3,5},{4,2},{5,3},{6,0},{7,1},{8,14},{9,15},{10,... | collective-permute-start | bytes 294920 | tf_op jit(solution)/shard_map/ppermute | solution.py:21
  309.7 11.0 %collective-permute-start.30 = (bf16[1,2,12,2048]{3,1,2,0:T(2,128)(2,1)S(1)}, bf16[1,2,12,2048]{3,1,2,0:T(2,128)(2,1)S(1)}, u32[]{:S(2)}, u32[]{:S(2)}) collective-permute-start(bf16[1,2,12,2048]{3,1,2,0:T(2,128)(2,1)S(1)} %bitcast.719), channel_id=1, source_target_pairs={{0,7},{1,6},{2,5},{3,4},{4,3},{5,2},{6,1},{7,0},{8,15},{9,14},{10,... | collective-permute-start | bytes 294920 | tf_op jit(solution)/shard_map/ppermute | solution.py:21
  346.9 26.5 %all-to-all-start.4 = ((bf16[8,2,12,2048]{3,1,2,0:T(2,128)(2,1)}), bf16[8,2,12,2048]{3,1,2,0:T(2,128)(2,1)S(1)}, u32[]{:S(2)}, u32[]{:S(2)}) async-start(bf16[8,2,12,2048]{3,1,2,0:T(2,128)(2,1)} %copy.260), calls=%async_computation.4 | async-start | bytes 1572864 | tf_op jit(solution)/shard_map/all_to_all | solution.py:81
  386.7 15.0 %collective-permute-start.35 = (bf16[1,2,12,2048]{3,1,2,0:T(2,128)(2,1)S(1)}, bf16[1,2,12,2048]{3,1,2,0:T(2,128)(2,1)S(1)}, u32[]{:S(2)}, u32[]{:S(2)}) collective-permute-start(bf16[1,2,12,2048]{3,1,2,0:T(2,128)(2,1)S(1)} %bitcast.732), channel_id=1, source_target_pairs={{0,4},{1,5},{2,6},{3,7},{4,0},{5,1},{6,2},{7,3},{8,12},{9,13},{10,... | collective-permute-start | bytes 294920 | tf_op jit(solution)/shard_map/ppermute | solution.py:21
  387.0 15.6 %collective-permute-start.36 = (bf16[1,2,12,2048]{3,1,2,0:T(2,128)(2,1)S(1)}, bf16[1,2,12,2048]{3,1,2,0:T(2,128)(2,1)S(1)}, u32[]{:S(2)}, u32[]{:S(2)}) collective-permute-start(bf16[1,2,12,2048]{3,1,2,0:T(2,128)(2,1)S(1)} %bitcast.726), channel_id=1, source_target_pairs={{0,5},{1,4},{2,7},{3,6},{4,1},{5,0},{6,3},{7,2},{8,13},{9,12},{10,... | collective-permute-start | bytes 294920 | tf_op jit(solution)/shard_map/ppermute | solution.py:21
  390.4 12.3 %collective-permute-start.37 = (bf16[1,2,12,2048]{3,1,2,0:T(2,128)(2,1)S(1)}, bf16[1,2,12,2048]{3,1,2,0:T(2,128)(2,1)S(1)}, u32[]{:S(2)}, u32[]{:S(2)}) collective-permute-start(bf16[1,2,12,2048]{3,1,2,0:T(2,128)(2,1)S(1)} %bitcast.744), channel_id=1, source_target_pairs={{0,6},{1,7},{2,4},{3,5},{4,2},{5,3},{6,0},{7,1},{8,14},{9,15},{10,... | collective-permute-start | bytes 294920 | tf_op jit(solution)/shard_map/ppermute | solution.py:21
  429.0 26.7 %all-to-all-start.5 = ((bf16[8,2,12,2048]{3,1,2,0:T(2,128)(2,1)}), bf16[8,2,12,2048]{3,1,2,0:T(2,128)(2,1)S(1)}, u32[]{:S(2)}, u32[]{:S(2)}) async-start(bf16[8,2,12,2048]{3,1,2,0:T(2,128)(2,1)} %copy.282), calls=%async_computation.5 | async-start | bytes 1572864 | tf_op jit(solution)/shard_map/all_to_all | solution.py:81
  469.1 15.0 %collective-permute-start.43 = (bf16[1,2,12,2048]{3,1,2,0:T(2,128)(2,1)S(1)}, bf16[1,2,12,2048]{3,1,2,0:T(2,128)(2,1)S(1)}, u32[]{:S(2)}, u32[]{:S(2)}) collective-permute-start(bf16[1,2,12,2048]{3,1,2,0:T(2,128)(2,1)S(1)} %bitcast.733), channel_id=1, source_target_pairs={{0,4},{1,5},{2,6},{3,7},{4,0},{5,1},{6,2},{7,3},{8,12},{9,13},{10,... | collective-permute-start | bytes 294920 | tf_op jit(solution)/shard_map/ppermute | solution.py:21
  469.3 15.6 %collective-permute-start.44 = (bf16[1,2,12,2048]{3,1,2,0:T(2,128)(2,1)S(1)}, bf16[1,2,12,2048]{3,1,2,0:T(2,128)(2,1)S(1)}, u32[]{:S(2)}, u32[]{:S(2)}) collective-permute-start(bf16[1,2,12,2048]{3,1,2,0:T(2,128)(2,1)S(1)} %bitcast.727), channel_id=1, source_target_pairs={{0,5},{1,4},{2,7},{3,6},{4,1},{5,0},{6,3},{7,2},{8,13},{9,12},{10,... | collective-permute-start | bytes 294920 | tf_op jit(solution)/shard_map/ppermute | solution.py:21
  472.8 12.3 %collective-permute-start.45 = (bf16[1,2,12,2048]{3,1,2,0:T(2,128)(2,1)S(1)}, bf16[1,2,12,2048]{3,1,2,0:T(2,128)(2,1)S(1)}, u32[]{:S(2)}, u32[]{:S(2)}) collective-permute-start(bf16[1,2,12,2048]{3,1,2,0:T(2,128)(2,1)S(1)} %bitcast.745), channel_id=1, source_target_pairs={{0,6},{1,7},{2,4},{3,5},{4,2},{5,3},{6,0},{7,1},{8,14},{9,15},{10,... | collective-permute-start | bytes 294920 | tf_op jit(solution)/shard_map/ppermute | solution.py:21
  474.2 11.0 %collective-permute-start.46 = (bf16[1,2,12,2048]{3,1,2,0:T(2,128)(2,1)S(1)}, bf16[1,2,12,2048]{3,1,2,0:T(2,128)(2,1)S(1)}, u32[]{:S(2)}, u32[]{:S(2)}) collective-permute-start(bf16[1,2,12,2048]{3,1,2,0:T(2,128)(2,1)S(1)} %bitcast.721), channel_id=1, source_target_pairs={{0,7},{1,6},{2,5},{3,4},{4,3},{5,2},{6,1},{7,0},{8,15},{9,14},{10,... | collective-permute-start | bytes 294920 | tf_op jit(solution)/shard_map/ppermute | solution.py:21
  511.3 26.5 %all-to-all-start.6 = ((bf16[8,2,12,2048]{3,1,2,0:T(2,128)(2,1)}), bf16[8,2,12,2048]{3,1,2,0:T(2,128)(2,1)S(1)}, u32[]{:S(2)}, u32[]{:S(2)}) async-start(bf16[8,2,12,2048]{3,1,2,0:T(2,128)(2,1)} %copy.304), calls=%async_computation.6 | async-start | bytes 1572864 | tf_op jit(solution)/shard_map/all_to_all | solution.py:81
  551.1 15.0 %collective-permute-start.51 = (bf16[1,2,12,2048]{3,1,2,0:T(2,128)(2,1)S(1)}, bf16[1,2,12,2048]{3,1,2,0:T(2,128)(2,1)S(1)}, u32[]{:S(2)}, u32[]{:S(2)}) collective-permute-start(bf16[1,2,12,2048]{3,1,2,0:T(2,128)(2,1)S(1)} %bitcast.713), channel_id=1, source_target_pairs={{0,4},{1,5},{2,6},{3,7},{4,0},{5,1},{6,2},{7,3},{8,12},{9,13},{10,... | collective-permute-start | bytes 294920 | tf_op jit(solution)/shard_map/ppermute | solution.py:21
  551.4 15.7 %collective-permute-start.52 = (bf16[1,2,12,2048]{3,1,2,0:T(2,128)(2,1)S(1)}, bf16[1,2,12,2048]{3,1,2,0:T(2,128)(2,1)S(1)}, u32[]{:S(2)}, u32[]{:S(2)}) collective-permute-start(bf16[1,2,12,2048]{3,1,2,0:T(2,128)(2,1)S(1)} %bitcast.712), channel_id=1, source_target_pairs={{0,5},{1,4},{2,7},{3,6},{4,1},{5,0},{6,3},{7,2},{8,13},{9,12},{10,... | collective-permute-start | bytes 294920 | tf_op jit(solution)/shard_map/ppermute | solution.py:21
  554.8 12.3 %collective-permute-start.53 = (bf16[1,2,12,2048]{3,1,2,0:T(2,128)(2,1)S(1)}, bf16[1,2,12,2048]{3,1,2,0:T(2,128)(2,1)S(1)}, u32[]{:S(2)}, u32[]{:S(2)}) collective-permute-start(bf16[1,2,12,2048]{3,1,2,0:T(2,128)(2,1)S(1)} %bitcast.715), channel_id=1, source_target_pairs={{0,6},{1,7},{2,4},{3,5},{4,2},{5,3},{6,0},{7,1},{8,14},{9,15},{10,... | collective-permute-start | bytes 294920 | tf_op jit(solution)/shard_map/ppermute | solution.py:21
  556.3 11.0 %collective-permute-start.54 = (bf16[1,2,12,2048]{3,1,2,0:T(2,128)(2,1)S(1)}, bf16[1,2,12,2048]{3,1,2,0:T(2,128)(2,1)S(1)}, u32[]{:S(2)}, u32[]{:S(2)}) collective-permute-start(bf16[1,2,12,2048]{3,1,2,0:T(2,128)(2,1)S(1)} %bitcast.711), channel_id=1, source_target_pairs={{0,7},{1,6},{2,5},{3,4},{4,3},{5,2},{6,1},{7,0},{8,15},{9,14},{10,... | collective-permute-start | bytes 294920 | tf_op jit(solution)/shard_map/ppermute | solution.py:21
  (33 other events, 311.3 us)
